TPU v7x, 32 devices: a whole 2x2x4 slice. The times are simulated.
32 devices in a mesh: tm: 8 (over z, y), rows: 4 (over x, core).
Axes of the slice: x: 2, y: 2, z: 4, core: 2. Of those that a mesh axis runs over, the one named last changes fastest.
Arguments:
- pivot_blocks: float32 [8, 512, 512], P('tm'), may hold values from -4 to 24, as said below
- lower_blocks: float32 [8, 512, 512], P('tm', None, 'rows'), may hold values from -5 to 0.5
- top_diagonal: float32 [8, 512, 512], P('tm', 'rows'), may hold values from -1 to 2, as said below
- top_coupling: float32 [8, 512, 512], P('tm', 'rows'), may hold values from -3 to 3
Outputs:
- sigma_diagonal: float32 [8, 512, 512], P('tm', 'rows')
- sigma_next: float32 [8, 512, 512], P('tm', 'rows')
- reduced_pivot: float32 [8, 512, 512], P('tm', 'rows')
Inputs may be any that keep to these rules, and one draw needn't show every extreme that they name: `pivot_blocks`: each block is symmetric, and the block-tridiagonal matrix with these diagonal blocks and the couplings lower_blocks is positive definite. `top_diagonal`: each block is symmetric.
All inputs are finite; a program needn't handle non-finite values.
Results may differ from a plain program's by a relative error of at most 0.0001.
Values sent between devices are 32-bit elements; how exact they have to be, the bound alone decides.
No kernel may reach another device: no remote copies, remote signals or barrier semaphores. Data moves between devices by JAX's collectives and lax.ppermute only.
A program may use at most 64 MiB of HBM per device.

v0:
```python
import jax
import jax.numpy as jnp
from jax import lax
from jax.sharding import PartitionSpec as P

LEVELS = 2


precise = lax.Precision.HIGHEST


def passed_along(value, axis, steps):
    count = lax.axis_size(axis)
    leading, last = (max(0, -steps), min(count, count - steps))
    return lax.ppermute(value, axis, [(source, source + steps) for source in range(leading, last)])


def product(left, right):
    return jnp.dot(left, right, precision=precise, preferred_element_type=jnp.float32)


def product_flip(left, right):
    return lax.dot_general(
        left, right, (((1,), (1,)), ((), ())), precision=precise, preferred_element_type=jnp.float32
    )


def product_over(left, right):
    return lax.dot_general(
        left, right, (((0,), (0,)), ((), ())), precision=precise, preferred_element_type=jnp.float32
    )


def solve_with(factor, right_side):
    return jax.scipy.linalg.cho_solve((factor, True), right_side)


def local(pivot_blocks, lower_blocks, top_diagonal, top_coupling):
    parts_count = lax.axis_size("tm")
    position = lax.axis_index("tm")
    row_part = lax.axis_index("rows")
    full_width = pivot_blocks.shape[1]
    quarter = lower_blocks.shape[2]
    row_start = row_part * quarter
    first_pivot = pivot_blocks[0]
    lower_columns = jnp.where(position == 0, jnp.zeros_like(lower_blocks[0]), lower_blocks[0])
    lower_rows = lax.all_to_all(lower_columns, "rows", split_axis=0, concat_axis=1, tiled=True)
    next_rows = passed_along(lower_rows, "tm", -1)
    upper_columns = next_rows.T
    pivot_rows = lax.dynamic_slice_in_dim(first_pivot, row_start, quarter, 0)
    unit_columns = (
        jnp.arange(full_width)[:, None] == row_start + jnp.arange(quarter)[None, :]
    ).astype(jnp.float32)
    saved = []
    for tier_index in range(LEVELS):
        spacing = 2**tier_index
        if tier_index == 0:
            whole_pivot = first_pivot
        else:
            whole_pivot = lax.all_gather(pivot_rows, "rows", axis=0, tiled=True)
        factor = jnp.linalg.cholesky(whole_pivot)
        solved = solve_with(
            factor, jnp.concatenate([lower_columns, upper_columns, unit_columns], axis=1)
        )
        left_columns = solved[:, :quarter]
        right_columns = solved[:, quarter : 2 * quarter]
        inverse_columns = solved[:, 2 * quarter :]
        left_solved, right_solved = (
            lax.all_gather(left_columns, "rows", axis=1, tiled=True),
            lax.all_gather(right_columns, "rows", axis=1, tiled=True),
        )
        drop_left = product_over(lower_columns, left_solved)
        upper_new = -product_over(upper_columns, left_solved)
        left_bound = passed_along(jnp.stack([drop_left, upper_new]), "tm", -spacing)
        drop_right = product_over(upper_columns, right_solved)
        lower_new = -product_over(lower_columns, right_solved)
        right_bound = passed_along(jnp.stack([drop_right, lower_new]), "tm", spacing)
        pivot_rows = pivot_rows - left_bound[0] - right_bound[0]
        upper_columns = left_bound[1].T
        lower_columns = right_bound[1].T
        saved.append((left_solved, right_solved, inverse_columns))
    diagonal_rows = top_diagonal[0]
    coupling_rows = jnp.where(
        position + 2**LEVELS >= parts_count, jnp.zeros_like(top_coupling[0]), top_coupling[0]
    )
    for tier_index in reversed(range(LEVELS)):
        spacing = 2**tier_index
        saved_left, saved_right, saved_inverse = saved[tier_index]
        left_rows = lax.dynamic_slice_in_dim(saved_left, row_start, quarter, 0)
        right_rows = lax.dynamic_slice_in_dim(saved_right, row_start, quarter, 0)
        from_left = passed_along(jnp.stack([diagonal_rows, coupling_rows]), "tm", spacing)
        from_right = passed_along(diagonal_rows, "tm", -spacing)
        joined = lax.all_gather(
            jnp.concatenate([from_left, from_right[None]], 0), "rows", axis=1, tiled=True
        )
        near_diagonal = joined[0]
        near_next = joined[1]
        far_diagonal = joined[2]
        cross_near = product(left_rows, near_diagonal) + product_flip(right_rows, near_next)
        cross_far = product(left_rows, near_next) + product(right_rows, far_diagonal)
        diagonal_rows = (
            saved_inverse.T
            + product_flip(cross_near, saved_left)
            + product_flip(cross_far, saved_right)
        )
        coupling_rows = -cross_far
    coupling_rows = jnp.where(
        position == parts_count - 1, jnp.zeros_like(coupling_rows), coupling_rows
    )
    return (diagonal_rows[None], coupling_rows[None], pivot_rows[None])


def solution(mesh):
    placed = (
        P("tm", None, None),
        P("tm", None, "rows"),
        P("tm", "rows", None),
        P("tm", "rows", None),
    )
    return jax.shard_map(
        local,
        mesh=mesh,
        in_specs=placed,
        out_specs=(P("tm", "rows", None), P("tm", "rows", None), P("tm", "rows", None)),
        check_vma=False,
    )
```

profile of v0, /device:TPU:24, one launch (start us, length us, event | category | flops | bytes accessed | tf_op | source)
XLA Modules:
  0.0 517.7 jit_solution(16746918872644759533)
XLA Ops:
  9.1 4.1 all-to-all-start
  13.2 1.6 copy.7
  15.0 11.7 %cholesky.286 = f32[128,128]{1,0:T(8,128)S(1)} custom-call(f32[128,128]{1,0:T(8,128)S(1)} %cholesky.426), custom_call_target="Cholesky" | custom-call | tf_op jit(solution)/shard_map/jit(cholesky)/cholesky | solution.py:61
  26.8 9.8 %custom-call.29 = f32[1,128,128]{1,2,0:T(8,128)S(1)} custom-call(f32[1,128,128]{2,1,0:T(8,128)S(1)} %get-tuple-element.70), custom_call_target="InvertDiagBlocksLowerTriangular" | custom-call | tf_op jit(solution)/shard_map/jit(cholesky)/cholesky | solution.py:61
  38.1 11.7 %cholesky.305 = f32[128,128]{1,0:T(8,128)S(1)} custom-call(f32[128,128]{1,0:T(8,128)S(1)} %cholesky.430), custom_call_target="Cholesky" | custom-call | tf_op jit(solution)/shard_map/jit(cholesky)/cholesky | solution.py:61
  49.8 10.2 %custom-call.30 = f32[1,128,128]{1,2,0:T(8,128)S(1)} custom-call(f32[1,128,128]{2,1,0:T(8,128)S(1)} %get-tuple-element.67), custom_call_target="InvertDiagBlocksLowerTriangular" | custom-call | tf_op jit(solution)/shard_map/jit(cholesky)/cholesky | solution.py:61
  62.3 13.2 %cholesky.326 = f32[128,128]{1,0:T(8,128)} custom-call(f32[128,128]{1,0:T(8,128)} %cholesky.435), custom_call_target="Cholesky" | custom-call | tf_op jit(solution)/shard_map/jit(cholesky)/cholesky | solution.py:61
  75.4 1.5 select_reduce_fusion.5
  77.6 11.3 %custom-call.31 = f32[1,128,128]{1,2,0:T(8,128)} custom-call(f32[1,128,128]{2,1,0:T(8,128)} %get-tuple-element.64), custom_call_target="InvertDiagBlocksLowerTriangular" | custom-call | tf_op jit(solution)/shard_map/jit(cholesky)/cholesky | solution.py:61
  90.3 11.7 %cholesky.343 = f32[128,128]{1,0:T(8,128)S(1)} custom-call(f32[128,128]{1,0:T(8,128)S(1)} %convolution_subtract_fusion.14), custom_call_target="Cholesky" | custom-call | tf_op jit(solution)/shard_map/jit(cholesky)/cholesky | solution.py:61
  106.1 8.0 %while.4 = (s32[]{:T(128)}, f32[512,512]{1,0:T(8,128)S(1)}, s32[4,2]{0,1:T(2,128)S(1)}, f32[4,128,128]{2,1,0:T(8,128)S(1)}, s32[]{:T(128)}) while((s32[]{:T(128)}, f32[512,512]{1,0:T(8,128)S(1)}, s32[4,2]{0,1:T(2,128)S(1)}, f32[4,128,128]{2,1,0:T(8,128)S(1)}, s32[]{:T(128)}) %tuple.60), condition=%wide.while_cond, body=%wide.while_body.sunk | while | flops 2 | bytes 131181 | solution.py:35
  106.7 1.4 bitcast_dynamic-update-slice_fusion.4
  108.7 1.4 bitcast_dynamic-update-slice_fusion.4
  110.7 1.4 bitcast_dynamic-update-slice_fusion.4
  112.7 1.4 bitcast_dynamic-update-slice_fusion.4
  114.9 3.3 collective-permute-start
  118.2 40.1 %custom-call.32 = f32[4,128,128]{1,2,0:T(8,128)S(1)} custom-call(f32[4,128,128]{2,1,0:T(8,128)} %copy-done.14), custom_call_target="InvertDiagBlocksLowerTriangular" | custom-call | tf_op jit(solution)/shard_map/jit(_cho_solve)/triangular_solve | solution.py:35
  166.6 16.7 %all-gather.9.cloned.1.call-done = f32[512,512]{1,0:T(8,128)} async-done(((f32[512,128]{1,0:T(8,128)}), f32[512,512]{1,0:T(8,128)}) %all-gather.9.cloned.1.call-update) | async-done | bytes 1048592 | tf_op jit(solution)/shard_map/all_gather | solution.py:69
  183.3 3.0 fusion.3
  186.3 3.0 convolution_bitcast_fusion.3
  190.2 3.3 collective-permute-start.1
  193.6 8.7 %all-gather.11.cloned.1.call-done = f32[512,512]{1,0:T(8,128)} async-done(((f32[512,128]{1,0:T(8,128)}), f32[512,512]{1,0:T(8,128)}) %all-gather.11.cloned.1.call-update) | async-done | bytes 1048592 | tf_op jit(solution)/shard_map/all_gather | solution.py:70
  202.3 3.0 convolution_bitcast_fusion.2
  205.3 3.0 fusion.2
  209.2 3.4 collective-permute-start.2
  212.6 13.7 %collective-permute-done.2 = f32[2,128,512]{1,2,0:T(8,128)S(1)} collective-permute-done((f32[2,128,512]{1,2,0:T(8,128)}, f32[2,128,512]{1,2,0:T(8,128)S(1)}, u32[]{:S(2)}, u32[]{:S(2)}) %collective-permute-start.2) | collective-permute-done | bytes 524320 | tf_op jit(solution)/shard_map/ppermute | solution.py:15
  229.6 4.6 collective-permute-start.4
  234.2 5.1 collective-permute-done.4
  239.3 4.1 collective-permute-done.3
  245.8 1.6 copy.15
  247.4 1.4 fusion.7
  248.9 11.7 %cholesky.358 = f32[128,128]{1,0:T(8,128)S(1)} custom-call(f32[128,128]{1,0:T(8,128)S(1)} %cholesky.439), custom_call_target="Cholesky" | custom-call | tf_op jit(solution)/shard_map/jit(cholesky)/cholesky | solution.py:61
  260.7 9.8 %custom-call.33 = f32[1,128,128]{1,2,0:T(8,128)S(1)} custom-call(f32[1,128,128]{2,1,0:T(8,128)S(1)} %get-tuple-element.60), custom_call_target="InvertDiagBlocksLowerTriangular" | custom-call | tf_op jit(solution)/shard_map/jit(cholesky)/cholesky | solution.py:61
  271.9 11.7 %cholesky.377 = f32[128,128]{1,0:T(8,128)S(1)} custom-call(f32[128,128]{1,0:T(8,128)S(1)} %cholesky.443), custom_call_target="Cholesky" | custom-call | tf_op jit(solution)/shard_map/jit(cholesky)/cholesky | solution.py:61
  285.1 10.0 %custom-call.34 = f32[1,128,128]{1,2,0:T(8,128)S(1)} custom-call(f32[1,128,128]{2,1,0:T(8,128)S(1)} %get-tuple-element.57), custom_call_target="InvertDiagBlocksLowerTriangular" | custom-call | tf_op jit(solution)/shard_map/jit(cholesky)/cholesky | solution.py:61
  297.2 13.2 %cholesky.398 = f32[128,128]{1,0:T(8,128)} custom-call(f32[128,128]{1,0:T(8,128)} %cholesky.448), custom_call_target="Cholesky" | custom-call | tf_op jit(solution)/shard_map/jit(cholesky)/cholesky | solution.py:61
  310.4 1.5 select_reduce_fusion.1
  312.5 11.3 %custom-call.35 = f32[1,128,128]{1,2,0:T(8,128)} custom-call(f32[1,128,128]{2,1,0:T(8,128)} %get-tuple-element.54), custom_call_target="InvertDiagBlocksLowerTriangular" | custom-call | tf_op jit(solution)/shard_map/jit(cholesky)/cholesky | solution.py:61
  325.3 11.7 %cholesky.415 = f32[128,128]{1,0:T(8,128)S(1)} custom-call(f32[128,128]{1,0:T(8,128)S(1)} %convolution_subtract_fusion.13), custom_call_target="Cholesky" | custom-call | tf_op jit(solution)/shard_map/jit(cholesky)/cholesky | solution.py:61
  340.6 8.0 %while.5 = (s32[]{:T(128)}, f32[512,512]{1,0:T(8,128)S(1)}, s32[4,2]{0,1:T(2,128)S(1)}, f32[4,128,128]{2,1,0:T(8,128)S(1)}, s32[]{:T(128)}) while((s32[]{:T(128)}, f32[512,512]{1,0:T(8,128)S(1)}, s32[4,2]{0,1:T(2,128)S(1)}, f32[4,128,128]{2,1,0:T(8,128)S(1)}, s32[]{:T(128)}) %tuple.80), condition=%wide.while_cond.clone, body=%wide.while_body.clone.sunk | while | flops 2 | bytes 131181 | solution.py:35
  341.2 1.4 bitcast_dynamic-update-slice_fusion.5
  343.2 1.4 bitcast_dynamic-update-slice_fusion.5
  345.2 1.4 bitcast_dynamic-update-slice_fusion.5
  348.6 39.3 %custom-call.36 = f32[4,128,128]{1,2,0:T(8,128)S(1)} custom-call(f32[4,128,128]{2,1,0:T(8,128)S(1)} %get-tuple-element.20), custom_call_target="InvertDiagBlocksLowerTriangular" | custom-call | tf_op jit(solution)/shard_map/jit(_cho_solve)/triangular_solve | solution.py:35
  392.6 1.5 convolution_subtract_fusion.3
  400.1 15.1 %all-gather.13.cloned.1.call-done = f32[512,512]{1,0:T(8,128)} async-done(((f32[512,128]{1,0:T(8,128)}), f32[512,512]{1,0:T(8,128)}) %all-gather.13.cloned.1.call-update) | async-done | bytes 1048592 | tf_op jit(solution)/shard_map/all_gather | solution.py:69
  415.1 3.9 fusion.9
  419.0 14.9 %all-gather.17.cloned.1.call-done = f32[512,512]{1,0:T(8,128)} async-done(((f32[512,128]{1,0:T(8,128)}), f32[512,512]{1,0:T(8,128)}) %all-gather.17.cloned.1.call-update) | async-done | bytes 1048592 | tf_op jit(solution)/shard_map/all_gather | solution.py:70
  434.0 3.2 convolution_add_fusion.5
  437.2 1.9 fusion.6
  439.2 2.4 convolution_add_fusion.7
  441.6 1.9 convolution_add_fusion.6
  444.6 3.4 collective-permute-start.5
  448.0 3.4 collective-permute-start.6
  451.4 15.7 %collective-permute-done.6 = f32[128,512]{0,1:T(8,128)S(1)} collective-permute-done((f32[128,512]{0,1:T(8,128)S(1)}, f32[128,512]{0,1:T(8,128)S(1)}, u32[]{:S(2)}, u32[]{:S(2)}) %collective-permute-start.6) | collective-permute-done | bytes 262176 | tf_op jit(solution)/shard_map/ppermute | solution.py:15
  468.1 1.8 convolution_bitcast_fusion.1
  469.9 2.8 fusion.1
  473.6 3.5 collective-permute-start.7
  477.1 2.8 convolution_bitcast_fusion
  479.9 1.8 fusion
  483.9 4.0 collective-permute-done.7
  487.8 10.5 %collective-permute-done.8 = f32[2,128,512]{1,2,0:T(8,128)} collective-permute-done((f32[2,128,512]{1,2,0:T(8,128)}, f32[2,128,512]{1,2,0:T(8,128)}, u32[]{:S(2)}, u32[]{:S(2)}) %collective-permute-start.8) | collective-permute-done | bytes 524320 | tf_op jit(solution)/shard_map/ppermute | solution.py:15
  500.3 2.5 fusion.10
  502.8 2.4 fusion.5
  (168 shorter events, 63.1 us)
Async XLA Ops:
  7.2 7.6 %copy-start.5 = (f32[1,512,512]{2,1,0:T(8,128)S(1)}, f32[1,512,512]{2,1,0:T(8,128)}, u32[]{:S(2)}) copy-start(f32[1,512,512]{2,1,0:T(8,128)} %param.7) | copy-start | bytes 3145732
  9.1 105.1 %all-to-all-start = ((f32[4,128,128]{1,2,0:T(8,128)}), f32[4,128,128]{1,2,0:T(8,128)}, u32[]{:S(2)}, u32[]{:S(2)}) async-start(f32[4,128,128]{1,2,0:T(8,128)} %copy.9), calls=%async_computation | async-start | bytes 524288 | tf_op jit(solution)/shard_map/all_to_all | solution.py:47
  13.1 170.2 %all-gather.9.cloned.1.call-start = ((), (), s32[]{:S(2)}) async-start(), calls=%async_computation.1 | async-start | bytes 1310720 | tf_op jit(solution)/shard_map/all_gather | solution.py:69
  37.4 0.7 copy-start.13
  114.1 0.7 copy-start.14
  114.9 44.5 %collective-permute-start = (f32[128,512]{0,1:T(8,128)}, f32[128,512]{0,1:T(8,128)S(1)}, u32[]{:S(2)}, u32[]{:S(2)}) collective-permute-start(f32[128,512]{0,1:T(8,128)} %bitcast.13), channel_id=1, source_target_pairs={{4,0},{8,4},{12,8},{16,12},{20,16},{24,20},{28,24},{5,1},{9,5},{13... | collective-permute-start | bytes 786440 | tf_op jit(solution)/shard_map/ppermute | solution.py:15
  165.8 36.5 %all-gather.11.cloned.1.call-start = ((), (), s32[]{:S(2)}) async-start(), calls=%async_computation.2 | async-start | bytes 1310720 | tf_op jit(solution)/shard_map/all_gather | solution.py:70
  166.6 79.3 %all-gather.21.cloned.1.call-start = ((), (), s32[]{:S(2)}) async-start(), calls=%async_computation.7 | async-start | bytes 1310720 | tf_op jit(solution)/shard_map/all_gather | solution.py:60
  190.2 22.3 %collective-permute-start.1 = (f32[2,128,512]{1,2,0:T(8,128)}, f32[2,128,512]{1,2,0:T(8,128)S(1)}, u32[]{:S(2)}, u32[]{:S(2)}) collective-permute-start(f32[2,128,512]{1,2,0:T(8,128)} %pad_maximum_fusion.6), channel_id=1, source_target_pairs={{4,0},{8,4},{12,8},{16,12},{20,16},{24,20},{28,24},{5,1},{9,5},{13... | collective-permute-start | bytes 1572872 | tf_op jit(solution)/shard_map/ppermute | solution.py:15
  209.2 17.1 %collective-permute-start.2 = (f32[2,128,512]{1,2,0:T(8,128)}, f32[2,128,512]{1,2,0:T(8,128)S(1)}, u32[]{:S(2)}, u32[]{:S(2)}) collective-permute-start(f32[2,128,512]{1,2,0:T(8,128)} %pad_maximum_fusion.7), channel_id=1, source_target_pairs={{0,4},{4,8},{8,12},{12,16},{16,20},{20,24},{24,28},{1,5},{5,9},{9,... | collective-permute-start | bytes 1572872 | tf_op jit(solution)/shard_map/ppermute | solution.py:15
  212.6 31.8 %copy-start.8 = (f32[2,128,512]{1,2,0:T(8,128)}, f32[2,128,512]{1,2,0:T(8,128)S(1)}, u32[]{:S(2)}) copy-start(f32[2,128,512]{1,2,0:T(8,128)S(1)} %collective-permute-done.1) | copy-start | bytes 1572868
  226.2 241.8 %copy-start.9 = (f32[2,128,512]{1,2,0:T(8,128)}, f32[2,128,512]{1,2,0:T(8,128)S(1)}, u32[]{:S(2)}) copy-start(f32[2,128,512]{1,2,0:T(8,128)S(1)} %collective-permute-done.2) | copy-start | bytes 1572868
  227.2 17.6 %copy-start.11 = (f32[512,128]{1,0:T(8,128)S(1)}, f32[512,128]{1,0:T(8,128)}, u32[]{:S(2)}) copy-start(f32[512,128]{1,0:T(8,128)} %get-tuple-element.50) | copy-start | bytes 786436
  227.2 172.8 %all-gather.15.cloned.1.call-start = ((), (), s32[]{:S(2)}) async-start(), calls=%async_computation.4 | async-start | bytes 3932160 | tf_op jit(solution)/shard_map/all_gather | solution.py:93
  228.3 15.1 %collective-permute-start.3 = (f32[2,128,512]{2,1,0:T(8,128)S(1)}, f32[2,128,512]{2,1,0:T(8,128)S(1)}, u32[]{:S(2)}, u32[]{:S(2)}) collective-permute-start(f32[2,128,512]{2,1,0:T(8,128)S(1)} %pad_maximum_fusion.8), channel_id=1, source_target_pairs={{0,8},{4,12},{8,16},{12,20},{16,24},{20,28},{1,9},{5,13},{9,17},{1... | collective-permute-start | bytes 1572872 | tf_op jit(solution)/shard_map/ppermute | solution.py:15
  229.6 9.7 %collective-permute-start.4 = (f32[128,512]{1,0:T(8,128)}, f32[128,512]{1,0:T(8,128)S(1)}, u32[]{:S(2)}, u32[]{:S(2)}) collective-permute-start(f32[128,512]{1,0:T(8,128)} %bitcast.220), channel_id=1, source_target_pairs={{8,0},{12,4},{16,8},{20,12},{24,16},{28,20},{9,1},{13,5},{17,9},{2... | collective-permute-start | bytes 786440 | tf_op jit(solution)/shard_map/ppermute | solution.py:15
  244.4 170.7 %all-gather.13.cloned.1.call-start = ((), (), s32[]{:S(2)}) async-start(), calls=%async_computation.3 | async-start | bytes 1310720 | tf_op jit(solution)/shard_map/all_gather | solution.py:69
  271.2 0.7 copy-start.12
  397.2 0.9 copy-start.6
  399.0 34.9 %all-gather.17.cloned.1.call-start = ((), (), s32[]{:S(2)}) async-start(), calls=%async_computation.5 | async-start | bytes 1310720 | tf_op jit(solution)/shard_map/all_gather | solution.py:70
  399.6 100.7 %all-gather.19.cloned.1.call-start = ((), (), s32[]{:S(2)}) async-start(), calls=%async_computation.6 | async-start | bytes 3932160 | tf_op jit(solution)/shard_map/all_gather | solution.py:93
  415.1 22.1 %copy-start.3 = (f32[512,512]{1,0:T(8,128)S(1)}, f32[512,512]{1,0:T(8,128)}, u32[]{:S(2)}) copy-start(f32[512,512]{1,0:T(8,128)} %all-gather.13.cloned.1.call-done) | copy-start | bytes 3145732
  434.0 5.2 %copy-start.2 = (f32[512,512]{1,0:T(8,128)S(1)}, f32[512,512]{1,0:T(8,128)}, u32[]{:S(2)}) copy-start(f32[512,512]{1,0:T(8,128)} %all-gather.17.cloned.1.call-done) | copy-start | bytes 3145732
  444.6 22.5 %collective-permute-start.5 = (f32[2,128,512]{1,2,0:T(8,128)S(1)}, f32[2,128,512]{1,2,0:T(8,128)S(1)}, u32[]{:S(2)}, u32[]{:S(2)}) collective-permute-start(f32[2,128,512]{1,2,0:T(8,128)S(1)} %pad_maximum_fusion.9), channel_id=1, source_target_pairs={{0,4},{4,8},{8,12},{12,16},{16,20},{20,24},{24,28},{1,5},{5,9},{9,... | collective-permute-start | bytes 1572872 | tf_op jit(solution)/shard_map/ppermute | solution.py:15
  448.0 19.1 %collective-permute-start.6 = (f32[128,512]{0,1:T(8,128)S(1)}, f32[128,512]{0,1:T(8,128)S(1)}, u32[]{:S(2)}, u32[]{:S(2)}) collective-permute-start(f32[128,512]{0,1:T(8,128)S(1)} %convolution_add_fusion.4), channel_id=1, source_target_pairs={{4,0},{8,4},{12,8},{16,12},{20,16},{24,20},{28,24},{5,1},{9,5},{13... | collective-permute-start | bytes 786440 | tf_op jit(solution)/shard_map/ppermute | solution.py:15
  469.9 10.0 %copy-start.10 = (f32[2,128,512]{1,2,0:T(8,128)S(1)}, f32[2,128,512]{1,2,0:T(8,128)}, u32[]{:S(2)}) copy-start(f32[2,128,512]{1,2,0:T(8,128)} %copy-done.9) | copy-start | bytes 1572868
  469.9 28.4 %copy-start.7 = (f32[1,128,512]{1,2,0:T(8,128)S(1)}, f32[1,128,512]{1,2,0:T(8,128)}, u32[]{:S(2)}) copy-start(f32[1,128,512]{1,2,0:T(8,128)} %get-tuple-element.48) | copy-start | bytes 786436
  473.6 26.7 %copy-start = (f32[512,512]{1,0:T(8,128)S(1)}, f32[512,512]{1,0:T(8,128)}, u32[]{:S(2)}) copy-start(f32[512,512]{1,0:T(8,128)} %all-gather.9.cloned.1.call-done) | copy-start | bytes 3145732
  473.6 14.2 %collective-permute-start.7 = (f32[2,128,512]{1,2,0:T(8,128)}, f32[2,128,512]{1,2,0:T(8,128)}, u32[]{:S(2)}, u32[]{:S(2)}) collective-permute-start(f32[2,128,512]{1,2,0:T(8,128)} %pad_maximum_fusion.10), channel_id=1, source_target_pairs={{8,0},{12,4},{16,8},{20,12},{24,16},{28,20},{9,1},{13,5},{17,9},{2... | collective-permute-start | bytes 1572872 | tf_op jit(solution)/shard_map/ppermute | solution.py:15
  481.7 23.5 %copy-start.1 = (f32[512,512]{1,0:T(8,128)S(1)}, f32[512,512]{1,0:T(8,128)}, u32[]{:S(2)}) copy-start(f32[512,512]{1,0:T(8,128)} %all-gather.11.cloned.1.call-done) | copy-start | bytes 3145732
  482.6 15.8 %collective-permute-start.8 = (f32[2,128,512]{1,2,0:T(8,128)}, f32[2,128,512]{1,2,0:T(8,128)}, u32[]{:S(2)}, u32[]{:S(2)}) collective-permute-start(f32[2,128,512]{1,2,0:T(8,128)} %pad_maximum_fusion.11), channel_id=1, source_target_pairs={{0,8},{4,12},{8,16},{12,20},{16,24},{20,28},{1,9},{5,13},{9,17},{1... | collective-permute-start | bytes 1572872 | tf_op jit(solution)/shard_map/ppermute | solution.py:15
  500.3 5.0 copy-start.4
Sparse Core Ops, SparseCore 0:
  165.9 17.3 all-gather.8
  185.4 16.8 all-gather.10
  227.4 15.9 all-gather.20
  244.7 28.5 all-gather.14
  399.1 15.9 all-gather.12
  417.1 16.8 all-gather.16
  468.2 27.9 all-gather.18
where the time goes:
time: 528 us; the launch traced here: 518 us
  other arithmetic  261 us (49%)
  waiting for transfers between devices  110 us (21%)
  matrix products  66.3 us (13%)
  starting transfers between devices  32.6 us (6%)
  local copies, waits for them, and re-layouts  27.7 us (5%)
  between operations  20.3 us (4%)
    another operation x29, other arithmetic, local(): factor = jnp.linalg.cholesky(whole_pivot)  167 us
    another operation x7, other arithmetic, solve_with(): return jax.scipy.linalg.cho_solve((factor, True), right_side)  80 us
    ppermute x9, waiting for transfers between devices, passed_along(): lax.ppermute(value, axis, [(source, source + steps) for source in range(l...  53.1 us
    all_gather x2, waiting for transfers between devices, local(): lax.all_gather(left_columns, 'rows', axis=1, tiled=True)  31.7 us
    ppermute x9, starting transfers between devices, passed_along(): lax.ppermute(value, axis, [(source, source + steps) for source in range(l...  27.4 us
    all_gather x2, waiting for transfers between devices, local(): lax.all_gather(right_columns, 'rows', axis=1, tiled=True)  23.6 us
    dot_general x8, matrix products, product_over(): lax.dot_general(left, right, (((0,), (0,)), ((), ())), precision=precise,...  21.3 us
    another operation x27, local copies, waits for them, and re-layouts, solve_with(): return jax.scipy.linalg.cho_solve((factor, True), right_side)  15.9 us
  transfers between devices with their start and end apart: 17, of which 10 were waited for; matrix products, arithmetic and copies ran while one was open for 62% of the time, Pallas kernels for 0%

commit v1 on v0

--- a/solution.py
+++ b/solution.py
@@ -2,6 +2,8 @@
 import jax.numpy as jnp
 from jax import lax
 from jax.sharding import PartitionSpec as P
+from jax.experimental import pallas as pl
+from jax.experimental.pallas import tpu as pltpu
 
 LEVELS = 2
 
@@ -31,8 +33,57 @@
     )
 
 
-def solve_with(factor, right_side):
-    return jax.scipy.linalg.cho_solve((factor, True), right_side)
+def small_inverse(block):
+    size = block.shape[0]
+    sub = lax.broadcasted_iota(jnp.int32, (size, size), 0)
+    lane = lax.broadcasted_iota(jnp.int32, (size, size), 1)
+    sub_col = lax.broadcasted_iota(jnp.int32, (size, 1), 0)
+    lane_row = lax.broadcasted_iota(jnp.int32, (1, size), 1)
+
+    def step(k, held):
+        row_mask = sub == k
+        col_mask = lane == k
+        row = jnp.sum(jnp.where(row_mask, held, 0.0), axis=0, keepdims=True)
+        col = jnp.sum(jnp.where(col_mask, held, 0.0), axis=1, keepdims=True)
+        pivot = jnp.sum(jnp.where(lane_row == k, row, 0.0), axis=1, keepdims=True)
+        scaled = jnp.where(lane_row == k, 1.0, row) / pivot
+        col = jnp.where(sub_col == k, 0.0, col)
+        held = jnp.where(col_mask, 0.0, held) - col * scaled
+        return jnp.where(row_mask, scaled, held)
+
+    return lax.fori_loop(0, size, step, block)
+
+
+def inverse_kernel(a_ref, o_ref):
+    n = a_ref.shape[0]
+    b = 128
+    o_ref[...] = a_ref[...]
+    sub_b = lax.broadcasted_iota(jnp.int32, (b, n), 0)
+    lane_b = lax.broadcasted_iota(jnp.int32, (b, n), 1)
+    sub_n = lax.broadcasted_iota(jnp.int32, (n, b), 0)
+    lane_n = lax.broadcasted_iota(jnp.int32, (n, n), 1)
+    for k in range(n // b):
+        lo = k * b
+        pivot_inv = small_inverse(o_ref[lo : lo + b, lo : lo + b])
+        in_block = (lane_b >= lo) & (lane_b < lo + b)
+        row_block = jnp.where(in_block, (lane_b - lo == sub_b).astype(jnp.float32), o_ref[lo : lo + b, :])
+        row_new = jnp.dot(pivot_inv, row_block, precision=precise, preferred_element_type=jnp.float32)
+        col_block = o_ref[:, lo : lo + b]
+        col_block = jnp.where((sub_n >= lo) & (sub_n < lo + b), 0.0, col_block)
+        whole = jnp.where((lane_n >= lo) & (lane_n < lo + b), 0.0, o_ref[...])
+        o_ref[...] = whole - jnp.dot(col_block, row_new, precision=precise, preferred_element_type=jnp.float32)
+        o_ref[lo : lo + b, :] = row_new
+
+
+def spd_inverse(matrix):
+    n = matrix.shape[0]
+    return pl.pallas_call(
+        inverse_kernel,
+        out_shape=jax.ShapeDtypeStruct((n, n), jnp.float32),
+        in_specs=[pl.BlockSpec(memory_space=pltpu.VMEM)],
+        out_specs=pl.BlockSpec(memory_space=pltpu.VMEM),
+        cost_estimate=pl.CostEstimate(flops=2 * n * n * n, bytes_accessed=8 * n * n, transcendentals=0),
+    )(matrix)
 
 
 def local(pivot_blocks, lower_blocks, top_diagonal, top_coupling):
@@ -48,9 +99,6 @@
     next_rows = passed_along(lower_rows, "tm", -1)
     upper_columns = next_rows.T
     pivot_rows = lax.dynamic_slice_in_dim(first_pivot, row_start, quarter, 0)
-    unit_columns = (
-        jnp.arange(full_width)[:, None] == row_start + jnp.arange(quarter)[None, :]
-    ).astype(jnp.float32)
     saved = []
     for tier_index in range(LEVELS):
         spacing = 2**tier_index
@@ -58,13 +106,11 @@
             whole_pivot = first_pivot
         else:
             whole_pivot = lax.all_gather(pivot_rows, "rows", axis=0, tiled=True)
-        factor = jnp.linalg.cholesky(whole_pivot)
-        solved = solve_with(
-            factor, jnp.concatenate([lower_columns, upper_columns, unit_columns], axis=1)
-        )
+        inverse_whole = spd_inverse(whole_pivot)
+        solved = product(inverse_whole, jnp.concatenate([lower_columns, upper_columns], axis=1))
         left_columns = solved[:, :quarter]
         right_columns = solved[:, quarter : 2 * quarter]
-        inverse_columns = solved[:, 2 * quarter :]
+        inverse_columns = lax.dynamic_slice_in_dim(inverse_whole, row_start, quarter, 1)
         left_solved, right_solved = (
             lax.all_gather(left_columns, "rows", axis=1, tiled=True),
             lax.all_gather(right_columns, "rows", axis=1, tiled=True),

time: 528 us -> 360 us (0.68)
  the two profiles are of different devices: /device:TPU:24 before, /device:TPU:0 now
where the time goes in v1:
time: 360 us; the launch traced here: 359 us
  Pallas kernels  137 us (38%)
  waiting for transfers between devices  117 us (32%)
  matrix products  44.5 us (12%)
  starting transfers between devices  25.4 us (7%)
  between operations  14.6 us (4%)
  blocking collectives  10 us (3%)
  other arithmetic  7.35 us (2%)
    pallas_call x2, Pallas kernels, spd_inverse(): pl.pallas_call(inverse_kernel, out_shape=jax.ShapeDtypeStruct((n, n), jnp...  137 us
    ppermute x9, waiting for transfers between devices, passed_along(): lax.ppermute(value, axis, [(source, source + steps) for source in range(l...  47.8 us
    all_gather x2, waiting for transfers between devices, local(): lax.all_gather(left_columns, 'rows', axis=1, tiled=True)  34.8 us
    all_gather x2, waiting for transfers between devices, local(): lax.all_gather(right_columns, 'rows', axis=1, tiled=True)  28.1 us
    ppermute x9, starting transfers between devices, passed_along(): lax.ppermute(value, axis, [(source, source + steps) for source in range(l...  24.9 us
    dot_general x8, matrix products, product(): jnp.dot(left, right, precision=precise, preferred_element_type=jnp.float32)  20 us
    dot_general x8, matrix products, product_over(): lax.dot_general(left, right, (((0,), (0,)), ((), ())), precision=precise,...  13.8 us
    dot_general x6, matrix products, product_flip(): lax.dot_general(left, right, (((1,), (1,)), ((), ())), precision=precise,...  10.7 us
  transfers between devices with their start and end apart: 16, of which 13 were waited for; matrix products, arithmetic and copies ran while one was open for 7% of the time, Pallas kernels for 38%

profile of v1, /device:TPU:0, one launch (start us, length us, event | category | flops | bytes accessed | tf_op | source)
XLA Modules:
  0.0 359.3 jit_solution(17674361198062193777)
XLA Ops:
  7.3 10.0 %all_to_all.16 = f32[4,128,128]{2,1,0:T(8,128)S(1)} all-to-all(f32[4,128,128]{2,1,0:T(8,128)S(1)} %bitcast.100), channel_id=1, replica_groups=mesh['tm'=8,'rows'=4] {'rows'}, dimensions={0} | all-to-all | bytes 524288 | tf_op jit(solution)/shard_map/all_to_all | solution.py:98
  17.3 0.1 copy.7
  17.4 1.3 collective-permute-start
  18.7 68.7 %shard_map.67 = f32[512,512]{1,0:T(8,128)} custom-call(f32[512,512]{1,0:T(8,128)} %bitcast.102), custom_call_target="tpu_custom_call" | custom-call | flops 268435456 | bytes 2097152 | tf_op jit(solution)/shard_map/pallas_call | solution.py:80
  87.4 3.1 convolution_bitcast_fusion
  90.5 0.8 fusion.45
  91.4 0.0 all-gather.11.cloned.1.call-start
  91.4 0.7 all-gather.11.cloned.1.call-update
  92.2 18.5 %all-gather.9.cloned.1.call-done = f32[512,512]{0,1:T(8,128)} async-done(((f32[512,128]{0,1:T(8,128)}), f32[512,512]{0,1:T(8,128)}) %all-gather.9.cloned.1.call-update) | async-done | bytes 1048592 | tf_op jit(solution)/shard_map/all_gather | solution.py:115
  110.7 2.5 fusion.3
  113.1 2.5 convolution_bitcast_fusion.4
  115.7 1.4 collective-permute-start.1
  117.1 12.4 %all-gather.11.cloned.1.call-done = f32[512,512]{0,1:T(8,128)} async-done(((f32[512,128]{0,1:T(8,128)}), f32[512,512]{0,1:T(8,128)}) %all-gather.11.cloned.1.call-update) | async-done | bytes 1048592 | tf_op jit(solution)/shard_map/all_gather | solution.py:116
  129.5 2.5 convolution_bitcast_fusion.3
  132.0 2.5 fusion.2
  134.6 3.4 collective-permute-start.2
  138.0 11.5 %collective-permute-done.2 = f32[2,128,512]{2,1,0:T(8,128)S(1)} collective-permute-done((f32[2,128,512]{2,1,0:T(8,128)S(1)}, f32[2,128,512]{2,1,0:T(8,128)S(1)}, u32[]{:S(2)}, u32[]{:S(2)}) %collective-permute-start.2) | collective-permute-done | bytes 524320 | tf_op jit(solution)/shard_map/ppermute | solution.py:17
  149.5 1.9 slice_bitcast_fusion.15
  151.5 0.0 all-gather.15.cloned.1.call-start
  151.6 5.3 %collective-permute-start.3 = (f32[2,128,512]{2,1,0:T(8,128)S(1)}, f32[2,128,512]{2,1,0:T(8,128)S(1)}, u32[]{:S(2)}, u32[]{:S(2)}) collective-permute-start(f32[2,128,512]{2,1,0:T(8,128)S(1)} %pad_maximum_fusion.4), channel_id=1, source_target_pairs={{0,8},{4,12},{8,16},{12,20},{16,24},{20,28},{1,9},{5,13},{9,17},{1... | collective-permute-start | bytes 1572872 | tf_op jit(solution)/shard_map/ppermute | solution.py:17
  156.9 1.3 collective-permute-start.4
  158.2 7.9 %collective-permute-done.4 = f32[128,512]{1,0:T(8,128)S(1)} collective-permute-done((f32[128,512]{1,0:T(8,128)S(1)}, f32[128,512]{1,0:T(8,128)S(1)}, u32[]{:S(2)}, u32[]{:S(2)}) %collective-permute-start.4) | collective-permute-done | bytes 262176 | tf_op jit(solution)/shard_map/ppermute | solution.py:17
  166.1 1.5 collective-permute-done.3
  167.6 1.0 pad_maximum_fusion
  168.6 0.2 all-gather.13.cloned.1.call-start
  168.8 0.5 all-gather.21.cloned.1.call-done
  169.3 68.7 %shard_map.68 = f32[512,512]{1,0:T(8,128)} custom-call(f32[512,512]{1,0:T(8,128)} %bitcast.103), custom_call_target="tpu_custom_call" | custom-call | flops 268435456 | bytes 2097152 | tf_op jit(solution)/shard_map/pallas_call | solution.py:80
  238.0 2.2 fusion.12
  240.2 0.8 fusion.44
  241.1 0.0 all-gather.17.cloned.1.call-start
  241.1 0.5 all-gather.17.cloned.1.call-update
  241.7 0.0 all-gather.19.cloned.1.call-start
  241.7 16.3 %all-gather.13.cloned.1.call-done = f32[512,512]{1,0:T(8,128)} async-done(((f32[512,128]{1,0:T(8,128)}), f32[512,512]{1,0:T(8,128)}) %all-gather.13.cloned.1.call-update) | async-done | bytes 1048592 | tf_op jit(solution)/shard_map/all_gather | solution.py:115
  258.1 3.2 fusion.7
  261.3 15.6 %all-gather.17.cloned.1.call-done = f32[512,512]{1,0:T(8,128)} async-done(((f32[512,128]{1,0:T(8,128)}), f32[512,512]{1,0:T(8,128)}) %all-gather.17.cloned.1.call-update) | async-done | bytes 1048592 | tf_op jit(solution)/shard_map/all_gather | solution.py:116
  276.9 3.2 convolution_add_fusion.5
  280.1 1.9 fusion.6
  282.1 2.4 convolution_add_fusion.7
  284.5 1.9 convolution_add_fusion.6
  286.4 1.0 convolution_add_fusion.4
  287.5 3.4 collective-permute-start.5
  290.9 1.3 collective-permute-start.6
  292.2 8.8 %collective-permute-done.6 = f32[128,512]{0,1:T(8,128)S(1)} collective-permute-done((f32[128,512]{0,1:T(8,128)S(1)}, f32[128,512]{0,1:T(8,128)S(1)}, u32[]{:S(2)}, u32[]{:S(2)}) %collective-permute-start.6) | collective-permute-done | bytes 262176 | tf_op jit(solution)/shard_map/ppermute | solution.py:17
  301.0 7.1 %collective-permute-done.5 = f32[2,128,512]{1,2,0:T(8,128)S(1)} collective-permute-done((f32[2,128,512]{1,2,0:T(8,128)S(1)}, f32[2,128,512]{1,2,0:T(8,128)S(1)}, u32[]{:S(2)}, u32[]{:S(2)}) %collective-permute-start.5) | collective-permute-done | bytes 524320 | tf_op jit(solution)/shard_map/ppermute | solution.py:17
  308.1 0.9 pad_maximum_fusion.1
  309.0 0.7 fusion.1
  309.7 0.7 convolution_bitcast_fusion.2
  310.5 0.8 pad_maximum_fusion.6
  311.3 1.3 collective-permute-start.7
  312.6 0.7 convolution_bitcast_fusion.1
  313.3 1.8 fusion
  315.1 6.2 %collective-permute-start.8 = (f32[2,128,512]{2,1,0:T(8,128)S(1)}, f32[2,128,512]{2,1,0:T(8,128)S(1)}, u32[]{:S(2)}, u32[]{:S(2)}) collective-permute-start(f32[2,128,512]{2,1,0:T(8,128)S(1)} %pad_maximum_fusion.7), channel_id=1, source_target_pairs={{0,8},{4,12},{8,16},{12,20},{16,24},{20,28},{1,9},{5,13},{9,17},{1... | collective-permute-start | bytes 1572872 | tf_op jit(solution)/shard_map/ppermute | solution.py:17
  321.3 7.7 %collective-permute-done.7 = f32[2,128,512]{2,1,0:T(8,128)} collective-permute-done((f32[2,128,512]{2,1,0:T(8,128)}, f32[2,128,512]{2,1,0:T(8,128)}, u32[]{:S(2)}, u32[]{:S(2)}) %collective-permute-start.7) | collective-permute-done | bytes 524320 | tf_op jit(solution)/shard_map/ppermute | solution.py:17
  329.0 3.4 collective-permute-done.8
  332.4 1.7 slice_subtract_fusion
  334.1 4.9 %all-gather.19.cloned.1.call-done = f32[3,512,512]{1,2,0:T(8,128)} async-done(((f32[3,128,512]{1,2,0:T(8,128)}), f32[3,512,512]{1,2,0:T(8,128)}) %all-gather.19.cloned.1.call-update) | async-done | bytes 3145744 | tf_op jit(solution)/shard_map/all_gather | solution.py:139
  339.1 2.6 fusion.8
  341.7 2.5 fusion.5
  344.2 1.3 convolution_add_fusion.1
  345.5 0.8 convolution_add_fusion.3
  346.3 2.8 convolution_add_fusion.2
  349.0 1.8 fusion.4
  350.8 0.8 copy.14
  351.7 0.7 select_bitcast_fusion
  (39 shorter events, 0.5 us)
Async XLA Ops:
  7.2 80.2 %copy-start.7 = (f32[1,512,128]{2,1,0:T(8,128)S(1)}, f32[1,512,128]{2,1,0:T(8,128)}, u32[]{:S(2)}) copy-start(f32[1,512,128]{2,1,0:T(8,128)} %param.5) | copy-start | bytes 786436
  7.2 103.5 %all-gather.9.cloned.1.call-start = ((), (), s32[]{:S(2)}) async-start(), calls=%async_computation.1 | async-start | bytes 1310720 | tf_op jit(solution)/shard_map/all_gather | solution.py:115
  17.4 70.0 %collective-permute-start = (f32[128,512]{0,1:T(8,128)S(1)}, f32[128,512]{0,1:T(8,128)S(1)}, u32[]{:S(2)}, u32[]{:S(2)}) collective-permute-start(f32[128,512]{0,1:T(8,128)S(1)} %bitcast.106), channel_id=1, source_target_pairs={{4,0},{8,4},{12,8},{16,12},{20,16},{24,20},{28,24},{5,1},{9,5},{13... | collective-permute-start | bytes 786440 | tf_op jit(solution)/shard_map/ppermute | solution.py:17
  91.4 38.1 %all-gather.11.cloned.1.call-start = ((), (), s32[]{:S(2)}) async-start(), calls=%async_computation.2 | async-start | bytes 1310720 | tf_op jit(solution)/shard_map/all_gather | solution.py:116
  92.1 77.2 %all-gather.21.cloned.1.call-start = ((), (), s32[]{:S(2)}) async-start(), calls=%async_computation.7 | async-start | bytes 1310720 | tf_op jit(solution)/shard_map/all_gather | solution.py:108
  115.7 35.9 %copy-start.8 = (f32[1,128,512]{2,1,0:T(8,128)S(1)}, f32[1,128,512]{2,1,0:T(8,128)}, u32[]{:S(2)}) copy-start(f32[1,128,512]{2,1,0:T(8,128)} %param.7) | copy-start | bytes 786436
  115.7 22.3 %collective-permute-start.1 = (f32[2,128,512]{2,1,0:T(8,128)S(1)}, f32[2,128,512]{2,1,0:T(8,128)S(1)}, u32[]{:S(2)}, u32[]{:S(2)}) collective-permute-start(f32[2,128,512]{2,1,0:T(8,128)S(1)} %pad_maximum_fusion.2), channel_id=1, source_target_pairs={{4,0},{8,4},{12,8},{16,12},{20,16},{24,20},{28,24},{5,1},{9,5},{13... | collective-permute-start | bytes 1572872 | tf_op jit(solution)/shard_map/ppermute | solution.py:17
  132.0 19.6 %copy-start.9 = (f32[1,128,512]{2,1,0:T(8,128)S(1)}, f32[1,128,512]{2,1,0:T(8,128)}, u32[]{:S(2)}) copy-start(f32[1,128,512]{2,1,0:T(8,128)} %param.6) | copy-start | bytes 786436
  134.6 14.9 %collective-permute-start.2 = (f32[2,128,512]{2,1,0:T(8,128)S(1)}, f32[2,128,512]{2,1,0:T(8,128)S(1)}, u32[]{:S(2)}, u32[]{:S(2)}) collective-permute-start(f32[2,128,512]{2,1,0:T(8,128)S(1)} %pad_maximum_fusion.3), channel_id=1, source_target_pairs={{0,4},{4,8},{8,12},{12,16},{16,20},{20,24},{24,28},{1,5},{5,9},{9,... | collective-permute-start | bytes 1572872 | tf_op jit(solution)/shard_map/ppermute | solution.py:17
  149.5 160.2 %copy-start.6 = (f32[2,128,512]{2,1,0:T(8,128)}, f32[2,128,512]{2,1,0:T(8,128)S(1)}, u32[]{:S(2)}) copy-start(f32[2,128,512]{2,1,0:T(8,128)S(1)} %collective-permute-done.2) | copy-start | bytes 1572868
  151.5 90.3 %all-gather.15.cloned.1.call-start = ((), (), s32[]{:S(2)}) async-start(), calls=%async_computation.4 | async-start | bytes 3932160 | tf_op jit(solution)/shard_map/all_gather | solution.py:139
  151.6 16.0 %collective-permute-start.3 = (f32[2,128,512]{2,1,0:T(8,128)S(1)}, f32[2,128,512]{2,1,0:T(8,128)S(1)}, u32[]{:S(2)}, u32[]{:S(2)}) collective-permute-start(f32[2,128,512]{2,1,0:T(8,128)S(1)} %pad_maximum_fusion.4), channel_id=1, source_target_pairs={{0,8},{4,12},{8,16},{12,20},{16,24},{20,28},{1,9},{5,13},{9,17},{1... | collective-permute-start | bytes 1572872 | tf_op jit(solution)/shard_map/ppermute | solution.py:17
  156.9 9.2 %collective-permute-start.4 = (f32[128,512]{1,0:T(8,128)S(1)}, f32[128,512]{1,0:T(8,128)S(1)}, u32[]{:S(2)}, u32[]{:S(2)}) collective-permute-start(f32[128,512]{1,0:T(8,128)S(1)} %bitcast.107), channel_id=1, source_target_pairs={{8,0},{12,4},{16,8},{20,12},{24,16},{28,20},{9,1},{13,5},{17,9},{2... | collective-permute-start | bytes 786440 | tf_op jit(solution)/shard_map/ppermute | solution.py:17
  168.6 89.5 %all-gather.13.cloned.1.call-start = ((), (), s32[]{:S(2)}) async-start(), calls=%async_computation.3 | async-start | bytes 1310720 | tf_op jit(solution)/shard_map/all_gather | solution.py:115
  241.1 35.8 %all-gather.17.cloned.1.call-start = ((), (), s32[]{:S(2)}) async-start(), calls=%async_computation.5 | async-start | bytes 1310720 | tf_op jit(solution)/shard_map/all_gather | solution.py:116
  241.7 97.4 %all-gather.19.cloned.1.call-start = ((), (), s32[]{:S(2)}) async-start(), calls=%async_computation.6 | async-start | bytes 3932160 | tf_op jit(solution)/shard_map/all_gather | solution.py:139
  258.1 22.1 %copy-start.3 = (f32[512,512]{1,0:T(8,128)S(1)}, f32[512,512]{1,0:T(8,128)}, u32[]{:S(2)}) copy-start(f32[512,512]{1,0:T(8,128)} %all-gather.13.cloned.1.call-done) | copy-start | bytes 3145732
  276.9 5.2 %copy-start.2 = (f32[512,512]{1,0:T(8,128)S(1)}, f32[512,512]{1,0:T(8,128)}, u32[]{:S(2)}) copy-start(f32[512,512]{1,0:T(8,128)} %all-gather.17.cloned.1.call-done) | copy-start | bytes 3145732
  287.5 20.6 %collective-permute-start.5 = (f32[2,128,512]{1,2,0:T(8,128)S(1)}, f32[2,128,512]{1,2,0:T(8,128)S(1)}, u32[]{:S(2)}, u32[]{:S(2)}) collective-permute-start(f32[2,128,512]{1,2,0:T(8,128)S(1)} %pad_maximum_fusion.5), channel_id=1, source_target_pairs={{0,4},{4,8},{8,12},{12,16},{16,20},{20,24},{24,28},{1,5},{5,9},{9,... | collective-permute-start | bytes 1572872 | tf_op jit(solution)/shard_map/ppermute | solution.py:17
  290.9 10.1 %collective-permute-start.6 = (f32[128,512]{0,1:T(8,128)S(1)}, f32[128,512]{0,1:T(8,128)S(1)}, u32[]{:S(2)}, u32[]{:S(2)}) collective-permute-start(f32[128,512]{0,1:T(8,128)S(1)} %convolution_add_fusion.4), channel_id=1, source_target_pairs={{4,0},{8,4},{12,8},{16,12},{20,16},{24,20},{28,24},{5,1},{9,5},{13... | collective-permute-start | bytes 786440 | tf_op jit(solution)/shard_map/ppermute | solution.py:17
  309.7 22.7 %copy-start.5 = (f32[1,128,512]{2,1,0:T(8,128)S(1)}, f32[1,128,512]{2,1,0:T(8,128)}, u32[]{:S(2)}) copy-start(f32[1,128,512]{2,1,0:T(8,128)} %get-tuple-element.9) | copy-start | bytes 786436
  310.5 28.6 %copy-start.1 = (f32[512,512]{0,1:T(8,128)S(1)}, f32[512,512]{0,1:T(8,128)}, u32[]{:S(2)}) copy-start(f32[512,512]{0,1:T(8,128)} %all-gather.9.cloned.1.call-done) | copy-start | bytes 3145732
  311.3 17.7 %collective-permute-start.7 = (f32[2,128,512]{2,1,0:T(8,128)}, f32[2,128,512]{2,1,0:T(8,128)}, u32[]{:S(2)}, u32[]{:S(2)}) collective-permute-start(f32[2,128,512]{2,1,0:T(8,128)} %pad_maximum_fusion.6), channel_id=1, source_target_pairs={{8,0},{12,4},{16,8},{20,12},{24,16},{28,20},{9,1},{13,5},{17,9},{2... | collective-permute-start | bytes 1572872 | tf_op jit(solution)/shard_map/ppermute | solution.py:17
  313.3 30.9 %copy-start = (f32[512,512]{0,1:T(8,128)S(1)}, f32[512,512]{0,1:T(8,128)}, u32[]{:S(2)}) copy-start(f32[512,512]{0,1:T(8,128)} %all-gather.11.cloned.1.call-done) | copy-start | bytes 3145732
  315.1 17.3 %collective-permute-start.8 = (f32[2,128,512]{2,1,0:T(8,128)S(1)}, f32[2,128,512]{2,1,0:T(8,128)S(1)}, u32[]{:S(2)}, u32[]{:S(2)}) collective-permute-start(f32[2,128,512]{2,1,0:T(8,128)S(1)} %pad_maximum_fusion.7), channel_id=1, source_target_pairs={{0,8},{4,12},{8,16},{12,20},{16,24},{20,28},{1,9},{5,13},{9,17},{1... | collective-permute-start | bytes 1572872 | tf_op jit(solution)/shard_map/ppermute | solution.py:17
  339.1 5.1 %copy-start.4 = (f32[3,512,512]{1,2,0:T(8,128)S(1)}, f32[3,512,512]{1,2,0:T(8,128)}, u32[]{:S(2)}) copy-start(f32[3,512,512]{1,2,0:T(8,128)} %all-gather.19.cloned.1.call-done) | copy-start | bytes 9437188
Sparse Core Ops, SparseCore 0:
  91.5 19.1 all-gather.8
  112.8 16.6 all-gather.10
  151.6 17.6 all-gather.20
  170.7 28.6 all-gather.14
  241.2 16.8 all-gather.12
  260.0 16.8 all-gather.16
  309.1 29.8 all-gather.18
